TPU v7x, 256 devices: a whole 4x4x8 slice. The times are simulated.
256 devices in a mesh: dp: 8 (over y, core), seq: 32 (over x, z).
Axes of the slice: x: 4, y: 4, z: 8, core: 2. Of those that a mesh axis runs over, the one named last changes fastest.
Arguments:
- queries: bfloat16 [16, 2048, 1536], P('dp', 'seq'), may hold values from -6 to 6
- key_rows: bfloat16 [16, 2048, 1536], P('dp', 'seq'), may hold values from -6 to 6
- value_rows: bfloat16 [16, 2048, 1536], P('dp', 'seq'), may hold values from -6 to 6
- layer_input: bfloat16 [16, 2048, 1536], P('dp', 'seq'), may hold values from -6 to 6
- utt_lengths: int32 [16], P('dp'), may hold values from 512 to 2048, as said below
- out_weight: bfloat16 [1536, 1536], replicated, may hold values from -0.15625 to 0.15625
- conv_kernel: bfloat16 [31, 1536], replicated, may hold values from -1 to 1
- conv_cotangent: bfloat16 [16, 2048, 1536], P('dp', 'seq'), may hold values from -6 to 6
- pick_weight: int32 [23592], replicated, may hold values from 0 to 2359295
- pick_kernel: int32 [476], replicated, may hold values from 0 to 47615
Outputs:
- conv_out: bfloat16 [16, 2048, 1536], P('dp', 'seq')
- context_grad: bfloat16 [16, 2048, 1536], P('dp', 'seq')
- weight_picks: float32 [23592], replicated
- kernel_picks: float32 [476], replicated
Inputs may be any that keep to these rules, and one draw needn't show every extreme that they name: `utt_lengths`: the first utterance fills all 2048 slots and the last has 512 valid frames.
All inputs are finite; a program needn't handle non-finite values.
Results may differ from a plain program's by a relative error of at most 0.0056.
Values may be sent and summed in bfloat16 or wider, within the bound.
No kernel may reach another device: no remote copies, remote signals or barrier semaphores. Data moves between devices by JAX's collectives and lax.ppermute only.
A program may use at most 128 MiB of HBM per device.

v0:
```python
import math

import jax
import jax.numpy as jnp
from jax import lax
from jax.sharding import PartitionSpec as P

HEADS = 16


neg_big = -1e30


def padded(value, sides, width):
    for axis, dim in sides:
        count, length = (lax.axis_size(axis), value.shape[dim])
        up = [(i, (i + 1) % count) for i in range(count - 1)]
        down = [(j, i) for i, j in up]
        last = lax.slice_in_dim(value, length - width, length, axis=dim)
        leading = lax.slice_in_dim(value, 0, width, axis=dim)
        before = lax.ppermute(last, axis, up)
        after = lax.ppermute(leading, axis, down)
        value = jnp.concatenate([before, value, after], axis=dim)
    return value


def softmax_rows(scores, key_ok):
    scores = jnp.where(key_ok, scores, neg_big)
    row_max = jnp.max(scores, axis=-1, keepdims=True)
    probs = jnp.exp(scores - row_max)
    return (probs.astype(jnp.bfloat16), jnp.sum(probs, axis=-1))


def pick_entries(table, picks):
    flat = table.reshape(-1)
    lane = math.gcd(flat.shape[0], 128)
    blocks = flat.reshape(flat.shape[0] // lane, lane)
    chosen = jnp.take(blocks, picks // lane, axis=0)
    lane_ids = jnp.arange(lane, dtype=jnp.int32)
    hit = lane_ids[None, :] == (picks % lane)[:, None]
    return jnp.sum(jnp.where(hit, chosen, jnp.float32(0.0)), axis=1)


def on_device(
    queries,
    key_rows,
    value_rows,
    layer_input,
    utt_lengths,
    out_weight,
    conv_kernel,
    conv_cotangent,
    pick_weight,
    pick_kernel,
):
    local_utts, frames_dev, width = queries.shape
    seq_count = lax.axis_size("seq")
    full_frames = frames_dev * seq_count
    head_size = width // HEADS
    score_scale = 1.0 / math.sqrt(head_size)
    first_frame = lax.axis_index("seq") * frames_dev
    local_ids = first_frame + jnp.arange(frames_dev, dtype=jnp.int32)
    valid_rows = (local_ids[None, :] < utt_lengths[:, None]).astype(jnp.float32)
    all_keys, all_values = (
        lax.all_gather(key_rows, "seq", axis=1, tiled=True),
        lax.all_gather(value_rows, "seq", axis=1, tiled=True),
    )
    full_ids = jnp.arange(full_frames, dtype=jnp.int32)

    def one_utt(item):
        query_utt, key_utt, value_utt, length_utt = item
        query_heads = query_utt.reshape(frames_dev, HEADS, head_size)
        key_heads = key_utt.reshape(full_frames, HEADS, head_size)
        value_heads = value_utt.reshape(full_frames, HEADS, head_size)
        scores = (
            jnp.einsum("qhd,khd->hqk", query_heads, key_heads, preferred_element_type=jnp.float32)
            * score_scale
        )
        weights, denom = softmax_rows(scores, (full_ids < length_utt)[None, None, :])
        out_rows = jnp.einsum(
            "hqk,khd->qhd", weights, value_heads, preferred_element_type=jnp.float32
        )
        out_rows = out_rows / denom.transpose(1, 0)[:, :, None]
        return out_rows.astype(jnp.bfloat16).reshape(frames_dev, width)

    context = lax.map(one_utt, (queries, all_keys, all_values, utt_lengths))
    context_flat = context.reshape(local_utts * frames_dev, width)
    projected = jnp.dot(context_flat, out_weight, preferred_element_type=jnp.float32).reshape(
        local_utts, frames_dev, width
    )
    hidden = ((layer_input.astype(jnp.float32) + projected) * valid_rows[:, :, None]).astype(
        jnp.bfloat16
    )
    tap_count = conv_kernel.shape[0]
    half_taps = (tap_count - 1) // 2
    kernel_f = conv_kernel.astype(jnp.float32)
    hidden_pad = padded(hidden, (("seq", 1),), half_taps)
    cot_f = conv_cotangent.astype(jnp.float32)
    conv_sum = jnp.zeros((local_utts, frames_dev, width), jnp.float32)
    kernel_rows = []
    for offset in range(tap_count):
        window = hidden_pad[:, offset : offset + frames_dev].astype(jnp.float32)
        conv_sum = conv_sum + kernel_f[offset] * window
        kernel_rows.append(jnp.sum(window * cot_f, axis=(0, 1)))
    conv_out = conv_sum.astype(jnp.bfloat16)
    kernel_grad = jnp.stack(kernel_rows)
    cot_pad = padded(conv_cotangent, (("seq", 1),), half_taps).astype(jnp.float32)
    back_sum = jnp.zeros((local_utts, frames_dev, width), jnp.float32)
    for offset in range(tap_count):
        begin = 2 * half_taps - offset
        back_sum = back_sum + kernel_f[offset] * cot_pad[:, begin : begin + frames_dev]
    hidden_grad = (back_sum * valid_rows[:, :, None]).astype(jnp.bfloat16)
    grad_flat = hidden_grad.reshape(local_utts * frames_dev, width)
    weight_grad = lax.dot_general(
        context_flat, grad_flat, (((0,), (0,)), ((), ())), preferred_element_type=jnp.float32
    )
    context_grad = lax.dot_general(
        grad_flat, out_weight, (((1,), (1,)), ((), ())), preferred_element_type=jnp.float32
    )
    context_grad = context_grad.reshape(local_utts, frames_dev, width).astype(jnp.bfloat16)
    weight_vals = pick_entries(weight_grad, pick_weight)
    kernel_vals = pick_entries(kernel_grad, pick_kernel)
    weight_sum, kernel_sum = lax.psum((weight_vals, kernel_vals), ("dp", "seq"))
    total_slots = local_utts * lax.axis_size("dp") * full_frames
    norm_factor = 1.0 / math.sqrt(total_slots)
    return (conv_out, context_grad, weight_sum * norm_factor, kernel_sum * norm_factor)


def solution(mesh):
    placed = (
        P("dp", "seq", None),
        P("dp", "seq", None),
        P("dp", "seq", None),
        P("dp", "seq", None),
        P("dp"),
        P(),
        P(),
        P("dp", "seq", None),
        P(),
        P(),
    )
    return jax.shard_map(
        on_device,
        mesh=mesh,
        in_specs=placed,
        out_specs=(P("dp", "seq", None), P("dp", "seq", None), P(), P()),
        check_vma=False,
    )
```

profile of v0, /device:TPU:16, one launch (start us, length us, event | category | flops | bytes accessed | tf_op | source)
XLA Modules:
  0.0 754.0 jit_solution(8033392045944065864)
XLA Ops:
  7.2 2.1 copy.22
  9.4 2.2 copy.23
  12.6 3.8 collective-permute-start.2
  27.9 3.3 fusion.104
  31.6 2.4 fusion.34
  34.0 99.6 %all-gather.3.cloned.1.call-done = bf16[2,2048,1536]{2,0,1:T(2,128)(2,1)} async-done(((bf16[2,64,1536]{2,0,1:T(2,128)(2,1)}), bf16[2,2048,1536]{2,0,1:T(2,128)(2,1)}) %all-gather.3.cloned.1.call-update) | async-done | bytes 12582928 | tf_op jit(solution)/shard_map/all_gather | solution.py:66
  133.6 31.1 %copy.24 = bf16[2,2048,1536]{1,2,0:T(8,128)(2,1)} copy(bf16[2,2048,1536]{2,0,1:T(2,128)(2,1)} %all-gather.3.cloned.1.call-done) | data formatting | bytes 25165824
  164.7 88.2 %all-gather.5.cloned.1.call-done = bf16[2,2048,1536]{2,0,1:T(2,128)(2,1)} async-done(((bf16[2,64,1536]{2,0,1:T(2,128)(2,1)}), bf16[2,2048,1536]{2,0,1:T(2,128)(2,1)}) %all-gather.5.cloned.1.call-update) | async-done | bytes 12582928 | tf_op jit(solution)/shard_map/all_gather | solution.py:65
  252.9 31.1 %copy.25 = bf16[2,2048,1536]{1,2,0:T(8,128)(2,1)} copy(bf16[2,2048,1536]{2,0,1:T(2,128)(2,1)} %all-gather.5.cloned.1.call-done) | data formatting | bytes 25165824
  284.1 51.8 %while.11 = (s32[]{:T(128)}, bf16[2,64,1536]{2,1,0:T(8,128)(2,1)S(1)}, bf16[2,2048,1536]{1,2,0:T(8,128)(2,1)}, s32[2]{0:T(128)S(1)}, bf16[2,64,1536]{2,1,0:T(8,1...) while((s32[]{:T(128)}, bf16[2,64,1536]{2,1,0:T(8,128)(2,1)S(1)}, ...), condition=%wide.region_3.4_spmd.clone, body=%wide.region_0.3_spmd.clone.sunk | while | flops 828571648 | bytes 65302632 | solution.py:86
  284.1 11.9 %constant_dynamic-slice_fusion.5 = (bf16[1,2048,1536]{1,2,0:T(8,128)(2,1)}, bf16[1,2048,1536]{1,2,0:T(8,128)(2,1)}) fusion(bf16[2,2048,1536]{1,2,0:T(8,128)(2,1)} %get-tuple-element.212, s32[]{:T(128)} %get-tuple-element.200, bf16[2,2048,1536]{1,2,0:T(8,128)(2,1)} %get-tuple-element.209), kind=kLoop, calls=%fused_computation.20.clone.1 | loop fusion | bytes 25165828 | tf_op jit(solution)/shard_map/while/body/jit(dynamic_index_in_dim)/dynamic_slice | solution.py:86
  297.5 5.0 fusion.182
  302.5 1.9 fusion.183
  304.4 5.1 fusion.184
  310.0 11.9 %constant_dynamic-slice_fusion.5 = (bf16[1,2048,1536]{1,2,0:T(8,128)(2,1)}, bf16[1,2048,1536]{1,2,0:T(8,128)(2,1)}) fusion(bf16[2,2048,1536]{1,2,0:T(8,128)(2,1)} %get-tuple-element.212, s32[]{:T(128)} %get-tuple-element.200, bf16[2,2048,1536]{1,2,0:T(8,128)(2,1)} %get-tuple-element.209), kind=kLoop, calls=%fused_computation.20.clone.1 | loop fusion | bytes 25165828 | tf_op jit(solution)/shard_map/while/body/jit(dynamic_index_in_dim)/dynamic_slice | solution.py:86
  323.4 5.0 fusion.182
  330.4 5.1 fusion.184
  335.9 5.0 convolution_bitcast_fusion
  341.8 10.5 %reshape_reshape.6 = f32[18432,128]{1,0:T(8,128)} reshape(f32[1536,1536]{1,0:T(8,128)} %convolution_bitcast_fusion) | data formatting | bytes 18874368 | tf_op jit(solution)/shard_map/reshape;reshape | solution.py:37
  352.3 48.0 %gather_fusion = f32[23592,128]{1,0:T(8,128)} fusion(f32[18432,128]{1,0:T(8,128)} %reshape_reshape.6, s32[24576]{0:T(1024)S(1)} %pad_clamp_fusion), kind=kCustom, calls=%fused_computation | custom fusion | bytes 24252576 | tf_op jit(solution)/shard_map/jit(_take)/gather | solution.py:38
  400.6 22.9 %select_reduce_fusion = f32[23592]{0:T(1024)} fusion(f32[23592,128]{1,0:T(8,128)} %gather_fusion, s32[23592]{0:T(1024)S(1)} %copy-done.2, pred[23592]{0:T(1024)(128)(4,1)S(1)} %copy-done.4), kind=kLoop, calls=%fused_computation.25 | loop fusion | flops 12055512 | bytes 12291432 | tf_op jit(solution)/shard_map/reduce_sum | solution.py:41
  426.6 234.2 %all-reduce.2.cloned.1.call-done = f32[23592]{0:T(1024)} async-done(((f32[23592]{0:T(1024)}), f32[23592]{0:T(1024)}) %all-reduce.2.cloned.1.call-update) | async-done | bytes 94384 | tf_op jit(solution)/shard_map/psum | solution.py:123
  668.9 73.1 %psum.15 = f32[476]{0:T(512)S(1)} all-reduce(f32[476]{0:T(512)S(1)} %select_reduce_fusion.1), channel_id=1, replica_groups=mesh['dp'=8,'seq'=32] {'dp','seq'}, use_global_device_ids=true, to_apply=%region_38.39 | all-reduce | flops 476 | bytes 3808 | tf_op jit(solution)/shard_map/psum | solution.py:123
  742.9 4.5 fusion.70
  (237 shorter events, 30.4 us)
Async XLA Ops:
  7.2 126.4 %all-gather.3.cloned.1.call-start = ((), (), s32[]{:S(2)}) async-start(), calls=%async_computation | async-start | bytes 12976128 | tf_op jit(solution)/shard_map/all_gather | solution.py:66
  9.4 243.6 %all-gather.5.cloned.1.call-start = ((), (), s32[]{:S(2)}) async-start(), calls=%async_computation.1 | async-start | bytes 12976128 | tf_op jit(solution)/shard_map/all_gather | solution.py:65
  11.6 649.2 %all-reduce.2.cloned.1.call-start = ((), (), s32[]{:S(2)}) async-start(), calls=%async_computation.2 | async-start | bytes 196608 | tf_op jit(solution)/shard_map/psum | solution.py:123
  12.6 13.9 %collective-permute-start.2 = (bf16[2,15,1536]{2,1,0:T(8,128)(2,1)S(1)}, bf16[2,15,1536]{2,1,0:T(8,128)(2,1)S(1)}, u32[]{:S(2)}, u32[]{:S(2)}) collective-permute-start(bf16[2,15,1536]{2,1,0:T(8,128)(2,1)S(1)} %get-tuple-element.144), channel_id=1, source_target_pairs={{0,1},{1,2},{2,3},{3,4},{4,5},{5,6},{6,7},{7,8},{8,9},{9,10},{10,1... | collective-permute-start | bytes 276488 | tf_op jit(solution)/shard_map/ppermute | solution.py:21
  16.5 10.1 %collective-permute-start.3 = (bf16[2,15,1536]{2,1,0:T(8,128)(2,1)S(1)}, bf16[2,15,1536]{2,1,0:T(8,128)(2,1)S(1)}, u32[]{:S(2)}, u32[]{:S(2)}) collective-permute-start(bf16[2,15,1536]{2,1,0:T(8,128)(2,1)S(1)} %get-tuple-element.145), channel_id=1, source_target_pairs={{1,0},{2,1},{3,2},{4,3},{5,4},{6,5},{7,6},{8,7},{9,8},{10,9},{11,1... | collective-permute-start | bytes 276488 | tf_op jit(solution)/shard_map/ppermute | solution.py:22
  400.3 342.3 %copy-start.6 = (f32[1536]{0:T(1024)S(1)}, f32[1536]{0:T(1024)}, u32[]{:S(2)}) copy-start(f32[1536]{0:T(1024)} %copy-done.5) | copy-start | bytes 18436
  400.3 342.3 %copy-start.8 = (f32[1536]{0:T(1024)S(1)}, f32[1536]{0:T(1024)}, u32[]{:S(2)}) copy-start(f32[1536]{0:T(1024)} %copy-done.7) | copy-start | bytes 18436
  400.3 342.3 %copy-start.10 = (f32[1536]{0:T(1024)S(1)}, f32[1536]{0:T(1024)}, u32[]{:S(2)}) copy-start(f32[1536]{0:T(1024)} %copy-done.9) | copy-start | bytes 18436
  400.4 342.3 %copy-start.12 = (f32[1536]{0:T(1024)S(1)}, f32[1536]{0:T(1024)}, u32[]{:S(2)}) copy-start(f32[1536]{0:T(1024)} %copy-done.11) | copy-start | bytes 18436
  400.4 342.3 %copy-start.14 = (f32[1536]{0:T(1024)S(1)}, f32[1536]{0:T(1024)}, u32[]{:S(2)}) copy-start(f32[1536]{0:T(1024)} %copy-done.13) | copy-start | bytes 18436
  400.4 342.3 %copy-start.16 = (f32[1536]{0:T(1024)S(1)}, f32[1536]{0:T(1024)}, u32[]{:S(2)}) copy-start(f32[1536]{0:T(1024)} %copy-done.15) | copy-start | bytes 18436
  400.4 342.3 %copy-start.18 = (f32[1536]{0:T(1024)S(1)}, f32[1536]{0:T(1024)}, u32[]{:S(2)}) copy-start(f32[1536]{0:T(1024)} %copy-done.17) | copy-start | bytes 18436
  400.4 342.3 %copy-start.20 = (f32[1536]{0:T(1024)S(1)}, f32[1536]{0:T(1024)}, u32[]{:S(2)}) copy-start(f32[1536]{0:T(1024)} %copy-done.19) | copy-start | bytes 18436
  400.4 342.3 %copy-start.22 = (f32[1536]{0:T(1024)S(1)}, f32[1536]{0:T(1024)}, u32[]{:S(2)}) copy-start(f32[1536]{0:T(1024)} %copy-done.21) | copy-start | bytes 18436
  400.4 342.3 %copy-start.24 = (f32[1536]{0:T(1024)S(1)}, f32[1536]{0:T(1024)}, u32[]{:S(2)}) copy-start(f32[1536]{0:T(1024)} %copy-done.23) | copy-start | bytes 18436
  400.4 342.3 %copy-start.26 = (f32[1536]{0:T(1024)S(1)}, f32[1536]{0:T(1024)}, u32[]{:S(2)}) copy-start(f32[1536]{0:T(1024)} %copy-done.25) | copy-start | bytes 18436
  400.4 342.3 %copy-start.28 = (f32[1536]{0:T(1024)S(1)}, f32[1536]{0:T(1024)}, u32[]{:S(2)}) copy-start(f32[1536]{0:T(1024)} %copy-done.27) | copy-start | bytes 18436
  400.4 342.3 %copy-start.30 = (f32[1536]{0:T(1024)S(1)}, f32[1536]{0:T(1024)}, u32[]{:S(2)}) copy-start(f32[1536]{0:T(1024)} %copy-done.29) | copy-start | bytes 18436
  400.5 342.3 %copy-start.32 = (f32[1536]{0:T(1024)S(1)}, f32[1536]{0:T(1024)}, u32[]{:S(2)}) copy-start(f32[1536]{0:T(1024)} %copy-done.31) | copy-start | bytes 18436
  400.5 342.3 %copy-start.34 = (f32[1536]{0:T(1024)S(1)}, f32[1536]{0:T(1024)}, u32[]{:S(2)}) copy-start(f32[1536]{0:T(1024)} %copy-done.33) | copy-start | bytes 18436
  400.5 342.3 %copy-start.36 = (f32[1536]{0:T(1024)S(1)}, f32[1536]{0:T(1024)}, u32[]{:S(2)}) copy-start(f32[1536]{0:T(1024)} %copy-done.35) | copy-start | bytes 18436
  400.5 342.3 %copy-start.38 = (f32[1536]{0:T(1024)S(1)}, f32[1536]{0:T(1024)}, u32[]{:S(2)}) copy-start(f32[1536]{0:T(1024)} %copy-done.37) | copy-start | bytes 18436
  423.6 238.8 %collective-permute-start = (bf16[2,15,1536]{2,1,0:T(8,128)(2,1)S(1)}, bf16[2,15,1536]{2,1,0:T(8,128)(2,1)S(1)}, u32[]{:S(2)}, u32[]{:S(2)}) collective-permute-start(bf16[2,15,1536]{2,1,0:T(8,128)(2,1)S(1)} %get-tuple-element.146), channel_id=1, source_target_pairs={{0,1},{1,2},{2,3},{3,4},{4,5},{5,6},{6,7},{7,8},{8,9},{9,10},{10,1... | collective-permute-start | bytes 276488 | tf_op jit(solution)/shard_map/ppermute | solution.py:21
  425.3 238.4 %collective-permute-start.1 = (bf16[2,15,1536]{2,1,0:T(8,128)(2,1)S(1)}, bf16[2,15,1536]{2,1,0:T(8,128)(2,1)S(1)}, u32[]{:S(2)}, u32[]{:S(2)}) collective-permute-start(bf16[2,15,1536]{2,1,0:T(8,128)(2,1)S(1)} %get-tuple-element.147), channel_id=1, source_target_pairs={{1,0},{2,1},{3,2},{4,3},{5,4},{6,5},{7,6},{8,7},{9,8},{10,9},{11,1... | collective-permute-start | bytes 276488 | tf_op jit(solution)/shard_map/ppermute | solution.py:22
  (58 other events, 6592.5 us)
Sparse Core Ops, SparseCore 0:
  11.2 122.4 all-gather.2
  136.2 116.7 all-gather.4
  423.7 237.1 all-reduce.1
where the time goes:
time: 759 us; the launch traced here: 754 us
  waiting for transfers between devices  422 us (56%)
  local copies, waits for them, and re-layouts  155 us (20%)
  blocking collectives  73.1 us (10%)
  other arithmetic  51.7 us (7%)
  matrix products  28.4 us (4%)
  between operations  15.2 us (2%)
  starting transfers between devices  8.23 us (1%)
    psum x1, waiting for transfers between devices, on_device(): weight_sum, kernel_sum = lax.psum((weight_vals, kernel_vals), ('dp', 'seq'))  234 us
    all_gather x1, waiting for transfers between devices, on_device(): lax.all_gather(value_rows, 'seq', axis=1, tiled=True)  99.6 us
    all_gather x1, waiting for transfers between devices, on_device(): lax.all_gather(key_rows, 'seq', axis=1, tiled=True)  88.2 us
    psum x1, blocking collectives, on_device(): weight_sum, kernel_sum = lax.psum((weight_vals, kernel_vals), ('dp', 'seq'))  73.1 us
    unnamed x154, local copies, waits for them, and re-layouts  66.9 us
    gather x2, local copies, waits for them, and re-layouts, pick_entries(): chosen = jnp.take(blocks, picks // lane, axis=0)  49.1 us
    dynamic_slice x6, local copies, waits for them, and re-layouts, on_device(): context = lax.map(one_utt, (queries, all_keys, all_values, utt_lengths))  25.1 us
    reduce_sum x2, other arithmetic, pick_entries(): return jnp.sum(jnp.where(hit, chosen, jnp.float32(0.0)), axis=1)  23.2 us
  transfers between devices with their start and end apart: 7, of which 3 were waited for; matrix products, arithmetic and copies ran while one was open for 7% of the time, Pallas kernels for 0%

commit v1 on v0

--- a/solution.py
+++ b/solution.py
@@ -41,6 +41,70 @@
     return jnp.sum(jnp.where(hit, chosen, jnp.float32(0.0)), axis=1)
 
 
+def butterfly_sum(value, axes):
+    for axis in axes:
+        count = lax.axis_size(axis)
+        step = 1
+        while step < count:
+            pairs = [(i, i ^ step) for i in range(count)]
+            value = value + lax.ppermute(value, axis, pairs)
+            step *= 2
+    return value
+
+
+def attend(query, key, value, key_ok, score_scale):
+    scores = jnp.dot(query, key.T, preferred_element_type=jnp.float32) * score_scale
+    weights, denom = softmax_rows(scores, key_ok[None, :])
+    out_rows = jnp.dot(weights, value, preferred_element_type=jnp.float32)
+    return (out_rows / denom[:, None]).astype(jnp.bfloat16)
+
+
+def head_attention(queries, key_rows, value_rows, utt_lengths, seq_index, score_scale):
+    local_utts, frames_dev, width = queries.shape
+    head_size = width // HEADS
+    seq_count = HEADS * local_utts
+    full_frames = frames_dev * seq_count
+    stacked = jnp.stack([queries, key_rows, value_rows])
+    stacked = stacked.reshape(3, local_utts, frames_dev, HEADS, head_size)
+    stacked = stacked.transpose(3, 1, 0, 2, 4).reshape(seq_count, 3, frames_dev, head_size)
+    gathered = lax.all_to_all(stacked, "seq", 0, 0, tiled=True)
+    gathered = gathered.transpose(1, 0, 2, 3).reshape(3, full_frames, head_size)
+    length = utt_lengths[seq_index % local_utts]
+    key_ok = jnp.arange(full_frames, dtype=jnp.int32) < length
+    out_rows = attend(gathered[0], gathered[1], gathered[2], key_ok, score_scale)
+    out_rows = out_rows.reshape(seq_count, frames_dev, head_size)
+    back = lax.all_to_all(out_rows, "seq", 0, 0, tiled=True)
+    back = back.reshape(HEADS, local_utts, frames_dev, head_size).transpose(1, 2, 0, 3)
+    return back.reshape(local_utts, frames_dev, width)
+
+
+def frame_attention(queries, key_rows, value_rows, utt_lengths, score_scale):
+    local_utts, frames_dev, width = queries.shape
+    head_size = width // HEADS
+    all_keys = lax.all_gather(key_rows, "seq", axis=1, tiled=True)
+    all_values = lax.all_gather(value_rows, "seq", axis=1, tiled=True)
+    full_frames = all_keys.shape[1]
+    full_ids = jnp.arange(full_frames, dtype=jnp.int32)
+
+    def one_utt(item):
+        query_utt, key_utt, value_utt, length_utt = item
+        query_heads = query_utt.reshape(frames_dev, HEADS, head_size)
+        key_heads = key_utt.reshape(full_frames, HEADS, head_size)
+        value_heads = value_utt.reshape(full_frames, HEADS, head_size)
+        scores = (
+            jnp.einsum("qhd,khd->hqk", query_heads, key_heads, preferred_element_type=jnp.float32)
+            * score_scale
+        )
+        weights, denom = softmax_rows(scores, (full_ids < length_utt)[None, None, :])
+        out_rows = jnp.einsum(
+            "hqk,khd->qhd", weights, value_heads, preferred_element_type=jnp.float32
+        )
+        out_rows = out_rows / denom.transpose(1, 0)[:, :, None]
+        return out_rows.astype(jnp.bfloat16).reshape(frames_dev, width)
+
+    return lax.map(one_utt, (queries, all_keys, all_values, utt_lengths))
+
+
 def on_device(
     queries,
     key_rows,
@@ -61,29 +125,11 @@
     first_frame = lax.axis_index("seq") * frames_dev
     local_ids = first_frame + jnp.arange(frames_dev, dtype=jnp.int32)
     valid_rows = (local_ids[None, :] < utt_lengths[:, None]).astype(jnp.float32)
-    all_keys, all_values = (
-        lax.all_gather(key_rows, "seq", axis=1, tiled=True),
-        lax.all_gather(value_rows, "seq", axis=1, tiled=True),
-    )
-    full_ids = jnp.arange(full_frames, dtype=jnp.int32)
-
-    def one_utt(item):
-        query_utt, key_utt, value_utt, length_utt = item
-        query_heads = query_utt.reshape(frames_dev, HEADS, head_size)
-        key_heads = key_utt.reshape(full_frames, HEADS, head_size)
-        value_heads = value_utt.reshape(full_frames, HEADS, head_size)
-        scores = (
-            jnp.einsum("qhd,khd->hqk", query_heads, key_heads, preferred_element_type=jnp.float32)
-            * score_scale
-        )
-        weights, denom = softmax_rows(scores, (full_ids < length_utt)[None, None, :])
-        out_rows = jnp.einsum(
-            "hqk,khd->qhd", weights, value_heads, preferred_element_type=jnp.float32
-        )
-        out_rows = out_rows / denom.transpose(1, 0)[:, :, None]
-        return out_rows.astype(jnp.bfloat16).reshape(frames_dev, width)
-
-    context = lax.map(one_utt, (queries, all_keys, all_values, utt_lengths))
+    seq_index = lax.axis_index("seq")
+    if HEADS * local_utts == seq_count:
+        context = head_attention(queries, key_rows, value_rows, utt_lengths, seq_index, score_scale)
+    else:
+        context = frame_attention(queries, key_rows, value_rows, utt_lengths, score_scale)
     context_flat = context.reshape(local_utts * frames_dev, width)
     projected = jnp.dot(context_flat, out_weight, preferred_element_type=jnp.float32).reshape(
         local_utts, frames_dev, width
@@ -120,7 +166,8 @@
     context_grad = context_grad.reshape(local_utts, frames_dev, width).astype(jnp.bfloat16)
     weight_vals = pick_entries(weight_grad, pick_weight)
     kernel_vals = pick_entries(kernel_grad, pick_kernel)
-    weight_sum, kernel_sum = lax.psum((weight_vals, kernel_vals), ("dp", "seq"))
+    joined = butterfly_sum(jnp.concatenate([weight_vals, kernel_vals]), ("dp", "seq"))
+    weight_sum, kernel_sum = joined[: weight_vals.shape[0]], joined[weight_vals.shape[0] :]
     total_slots = local_utts * lax.axis_size("dp") * full_frames
     norm_factor = 1.0 / math.sqrt(total_slots)
     return (conv_out, context_grad, weight_sum * norm_factor, kernel_sum * norm_factor)

time: 759 us -> 247 us (0.33)
  waiting for transfers between devices: 422 us -> 62 us
  local copies, waits for them, and re-layouts: 155 us -> 71.2 us
  blocking collectives: 73.1 us -> 0 us
  starting transfers between devices: 8.23 us -> 44 us
  between operations: 15.2 us -> 1.59 us
  matrix products: 28.4 us -> 20.8 us
    psum x1 -> x0, waiting for transfers between devices: 234 us -> none  [on_device(): weight_sum, kernel_sum = lax.psum((weight_vals, kernel_vals), ('dp', 'seq'))]
    all_gather x2 -> x0, waiting for transfers between devices: 188 us -> none  [the longest x1 99.6 us: on_device(): lax.all_gather(value_rows, 'seq', axis=1, tiled=True)]
    psum x1 -> x0, blocking collectives: 73.1 us -> none  [on_device(): weight_sum, kernel_sum = lax.psum((weight_vals, kernel_vals), ('dp', 'seq'))]
    unnamed x154 -> x62, local copies, waits for them, and re-layouts: 66.9 us -> 0.14 us
    ppermute x2, waiting for transfers between devices: 0.01 us -> 25.2 us  [padded(): after = lax.ppermute(leading, axis, down)]
    dynamic_slice x6 -> x1, local copies, waits for them, and re-layouts: 25.1 us -> 0.61 us  [head_attention(): length = utt_lengths[seq_index % local_utts]]
    ppermute x0 -> x8, waiting for transfers between devices: none -> 20.9 us  [butterfly_sum(): value = value + lax.ppermute(value, axis, pairs)]
    all_to_all x0 -> x2, starting transfers between devices: none -> 17.6 us  [the longest x1 11.3 us: head_attention(): gathered = lax.all_to_all(stacked, 'seq', 0, 0, tiled=True)]
  transfers between devices with their start and end apart: 7 -> 14, of which waited for: 3 -> 9; matrix products, arithmetic and copies ran while one was open for 7% -> 44% of each run, Pallas kernels for 0% -> 0%
where the time goes in v1:
time: 247 us; the launch traced here: 245 us
  local copies, waits for them, and re-layouts  71.2 us (29%)
  waiting for transfers between devices  62 us (25%)
  other arithmetic  45.8 us (19%)
  starting transfers between devices  44 us (18%)
  matrix products  20.8 us (8%)
    gather x2, local copies, waits for them, and re-layouts, pick_entries(): chosen = jnp.take(blocks, picks // lane, axis=0)  49.1 us
    ppermute x2, waiting for transfers between devices, padded(): after = lax.ppermute(leading, axis, down)  25.2 us
    reduce_sum x2, other arithmetic, pick_entries(): return jnp.sum(jnp.where(hit, chosen, jnp.float32(0.0)), axis=1)  22.5 us
    ppermute x8, waiting for transfers between devices, butterfly_sum(): value = value + lax.ppermute(value, axis, pairs)  20.9 us
    ppermute x8, starting transfers between devices, butterfly_sum(): value = value + lax.ppermute(value, axis, pairs)  13.6 us
    all_to_all x1, waiting for transfers between devices, head_attention(): back = lax.all_to_all(out_rows, 'seq', 0, 0, tiled=True)  13.3 us
    all_to_all x1, starting transfers between devices, head_attention(): gathered = lax.all_to_all(stacked, 'seq', 0, 0, tiled=True)  11.3 us
    another operation x2, local copies, waits for them, and re-layouts, pick_entries(): blocks = flat.reshape(flat.shape[0] // lane, lane)  10.5 us
  transfers between devices with their start and end apart: 14, of which 9 were waited for; matrix products, arithmetic and copies ran while one was open for 44% of the time, Pallas kernels for 0%

profile of v1, /device:TPU:16, one launch (start us, length us, event | category | flops | bytes accessed | tf_op | source)
XLA Modules:
  0.0 245.4 jit_solution(11694217805294708027)
XLA Ops:
  7.0 11.3 %all-to-all-start = ((bf16[32,3,64,96]{3,2,1,0:T(8,128)(2,1)}), bf16[32,3,64,96]{3,2,1,0:T(8,128)(2,1)S(1)}, u32[]{:S(2)}, u32[]{:S(2)}) async-start(bf16[32,3,64,96]{3,2,1,0:T(8,128)(2,1)} %bitcast.39), calls=%async_computation | async-start | bytes 3145728 | tf_op jit(solution)/shard_map/all_to_all | solution.py:70
  19.7 5.2 %collective-permute-start.2 = (bf16[2,15,1536]{2,1,0:T(8,128)(2,1)S(1)}, bf16[2,15,1536]{2,1,0:T(8,128)(2,1)}, u32[]{:S(2)}, u32[]{:S(2)}) collective-permute-start(bf16[2,15,1536]{2,1,0:T(8,128)(2,1)S(1)} %get-tuple-element.73), channel_id=1, source_target_pairs={{0,1},{1,2},{2,3},{3,4},{4,5},{5,6},{6,7},{7,8},{8,9},{9,10},{10,1... | collective-permute-start | bytes 276488 | tf_op jit(solution)/shard_map/ppermute | solution.py:21
  31.0 25.2 %collective-permute-done.3 = bf16[2,15,1536]{2,1,0:T(8,128)(2,1)S(1)} collective-permute-done((bf16[2,15,1536]{2,1,0:T(8,128)(2,1)S(1)}, bf16[2,15,1536]{2,1,0:T(8,128)(2,1)S(1)}, u32[]{:S(2)}, u32[]{:S(2)}) %collective-permute-start.3) | collective-permute-done | bytes 92192 | tf_op jit(solution)/shard_map/ppermute | solution.py:22
  57.3 2.5 %all-to-all-done = bf16[32,3,64,96]{3,2,1,0:T(8,128)(2,1)S(1)} async-done(((bf16[32,3,64,96]{3,2,1,0:T(8,128)(2,1)}), bf16[32,3,64,96]{3,2,1,0:T(8,128)(2,1)S(1)}, u32[]{:S(2)}, u32[]{:S(2)}) %all-to-all-start) | async-done | bytes 1179680 | tf_op jit(solution)/shard_map/all_to_all | solution.py:70
  59.9 4.0 %fusion = (f32[2048]{0:T(1024)S(1)}, f32[2048,2048]{0,1:T(8,128)S(1)}) fusion(pred[2048]{0:T(1024)(128)(4,1)} %iota_compare_fusion.2, bf16[2048,96]{1,0:T(8,128)(2,1)S(1)} %bitcast.43, bf16[2048,96]{1,0:T(8,128)(2,1)S(1)} %bitcast.45), kind=kOutput, calls=%fused_computation.4 | convolution fusion | flops 817887232 | bytes 17573888 | tf_op jit(solution)/shard_map/dot_general | solution.py:56
  63.9 4.9 %fusion.1 = f32[2048]{0:T(1024)S(1)} fusion(f32[2048,2048]{0,1:T(8,128)S(1)} %get-tuple-element.78, f32[2048]{0:T(1024)S(1)} %get-tuple-element.77, pred[2048]{0:T(1024)(128)(4,1)S(1)} %copy-done.24), kind=kLoop, calls=%fused_computation.5 | loop fusion | flops 16775168 | bytes 16795648 | tf_op jit(solution)/shard_map/reduce_sum | solution.py:31
  69.0 3.9 %fusion.25 = bf16[2048,96]{0,1:T(8,128)(2,1)S(1)} fusion(bf16[2048,96]{1,0:T(8,128)(2,1)S(1)} %bitcast.46, f32[2048,2048]{0,1:T(8,128)S(1)} %get-tuple-element.78, f32[2048]{0:T(1024)S(1)} %get-tuple-element.77, pred[2048]{0:T(1024)(128)(4,1)S(1)} %copy-done.24, f32[2048]{0:T(1024)S(1)} %fusion.1), kind=kOutput, calls=%fused_computation.79 | convolution fusion | flops 822476800 | bytes 17582080 | tf_op jit(solution)/shard_map/dot_general | solution.py:58
  73.9 6.3 %all-to-all-start.1 = ((bf16[32,64,96]{2,1,0:T(8,128)(2,1)}), bf16[32,64,96]{2,1,0:T(8,128)(2,1)S(1)}, u32[]{:S(2)}, u32[]{:S(2)}) async-start(bf16[32,64,96]{2,1,0:T(8,128)(2,1)} %bitcast.7), calls=%async_computation.1 | async-start | bytes 1048576 | tf_op jit(solution)/shard_map/all_to_all | solution.py:76
  80.5 3.1 %fusion.92 = bf16[2,64,1536]{2,1,0:T(8,128)(2,1)S(1)} fusion(f32[2,94,1536]{2,1,0:T(8,128)S(1)} %maximum_convert_fusion, f32[1536]{0:T(1024)S(1)} %get-tuple-element.36, f32[1536]{0:T(1024)S(1)} %get-tuple-element.37, f32[1536]{0:T(1024)S(1)} %get-tuple-element.38, f32[1536]{0:T(1024)S(1)} %get-tuple-element.39, f32[1536]{0:T(1024)S(1)} %get-tuple-element.40, ...), kind=kLoop, calls=%fused_computation.177 | loop fusion | flops 12386304 | bytes 24963584 | tf_op jit(solution)/shard_map/convert_element_type | solution.py:158
  83.6 13.3 %all-to-all-done.1 = bf16[32,64,96]{2,1,0:T(8,128)(2,1)S(1)} async-done(((bf16[32,64,96]{2,1,0:T(8,128)(2,1)}), bf16[32,64,96]{2,1,0:T(8,128)(2,1)S(1)}, u32[]{:S(2)}, u32[]{:S(2)}) %all-to-all-start.1) | async-done | bytes 393248 | tf_op jit(solution)/shard_map/all_to_all | solution.py:76
  98.4 3.1 %fusion.19 = bf16[2,64,1536]{2,1,0:T(8,128)(2,1)S(1)} fusion(bf16[2,64,1536]{2,1,0:T(8,128)(2,1)S(1)} %dot_general.19, bf16[1536,1536]{1,0:T(8,128)(2,1)} %param.15, bf16[2,64,1536]{2,1,0:T(8,128)(2,1)S(1)} %copy-done.1, f32[2,64]{1,0:T(2,128)S(1)} %copy-done.26), kind=kOutput, calls=%fused_computation.49 | convolution fusion | flops 604766208 | bytes 5898752 | tf_op jit(solution)/shard_map/dot_general | solution.py:134
  102.9 5.1 %collective-permute-start = (bf16[2,15,1536]{2,1,0:T(8,128)(2,1)S(1)}, bf16[2,15,1536]{2,1,0:T(8,128)(2,1)S(1)}, u32[]{:S(2)}, u32[]{:S(2)}) collective-permute-start(bf16[2,15,1536]{2,1,0:T(8,128)(2,1)S(1)} %get-tuple-element.75), channel_id=1, source_target_pairs={{0,1},{1,2},{2,3},{3,4},{4,5},{5,6},{6,7},{7,8},{8,9},{9,10},{10,1... | collective-permute-start | bytes 276488 | tf_op jit(solution)/shard_map/ppermute | solution.py:21
  108.0 5.0 %fusion.158 = f32[1536,1536]{1,0:T(8,128)} fusion(bf16[128,1536]{1,0:T(8,128)(2,1)S(1)} %reshape_reshape.9, bf16[128,1536]{1,0:T(8,128)(2,1)S(1)} %bitcast.40), kind=kOutput, calls=%fused_computation.335 | convolution fusion | flops 603979776 | bytes 10223616 | tf_op jit(solution)/shard_map/dot_general | solution.py:160
  113.0 10.5 %reshape_reshape.10 = f32[18432,128]{1,0:T(8,128)} reshape(f32[1536,1536]{1,0:T(8,128)} %fusion.158) | data formatting | bytes 18874368 | tf_op jit(solution)/shard_map/reshape;reshape | solution.py:37
  123.5 47.9 %gather_fusion = f32[23592,128]{1,0:T(8,128)} fusion(f32[18432,128]{1,0:T(8,128)} %reshape_reshape.10, s32[24576]{0:T(1024)S(1)} %pad_clamp_fusion), kind=kCustom, calls=%fused_computation | custom fusion | bytes 24252576 | tf_op jit(solution)/shard_map/jit(_take)/gather | solution.py:38
  171.5 22.2 %select_reduce_fusion = f32[23592]{0:T(1024)S(1)} fusion(f32[23592,128]{1,0:T(8,128)} %gather_fusion, s32[23592]{0:T(1024)S(1)} %add_select_fusion.1, pred[23592]{0:T(1024)(128)(4,1)S(1)} %get-tuple-element.66), kind=kLoop, calls=%fused_computation.7 | loop fusion | flops 12055512 | bytes 12291432 | tf_op jit(solution)/shard_map/reduce_sum | solution.py:41
  203.0 3.6 %collective-permute-done.5 = f32[24068]{0:T(1024)S(1)} collective-permute-done((f32[24068]{0:T(1024)S(1)}, f32[24068]{0:T(1024)S(1)}, u32[]{:S(2)}, u32[]{:S(2)}) %collective-permute-start.5) | collective-permute-done | bytes 96304 | tf_op jit(solution)/shard_map/ppermute | solution.py:50
  207.2 5.8 %collective-permute-done.6 = f32[24068]{0:T(1024)S(1)} collective-permute-done((f32[24068]{0:T(1024)S(1)}, f32[24068]{0:T(1024)S(1)}, u32[]{:S(2)}, u32[]{:S(2)}) %collective-permute-start.6) | collective-permute-done | bytes 96304 | tf_op jit(solution)/shard_map/ppermute | solution.py:50
  215.1 2.6 %collective-permute-done.7 = f32[24068]{0:T(1024)S(1)} collective-permute-done((f32[24068]{0:T(1024)S(1)}, f32[24068]{0:T(1024)S(1)}, u32[]{:S(2)}, u32[]{:S(2)}) %collective-permute-start.7) | collective-permute-done | bytes 96304 | tf_op jit(solution)/shard_map/ppermute | solution.py:50
  220.2 3.2 %collective-permute-done.8 = f32[24068]{0:T(1024)S(1)} collective-permute-done((f32[24068]{0:T(1024)S(1)}, f32[24068]{0:T(1024)S(1)}, u32[]{:S(2)}, u32[]{:S(2)}) %collective-permute-start.8) | collective-permute-done | bytes 96304 | tf_op jit(solution)/shard_map/ppermute | solution.py:50
  223.4 4.4 %collective-permute-start.9 = (f32[24068]{0:T(1024)S(1)}, f32[24068]{0:T(1024)S(1)}, u32[]{:S(2)}, u32[]{:S(2)}) collective-permute-start(f32[24068]{0:T(1024)S(1)} %add.329), channel_id=1, source_target_pairs={{0,4},{1,5},{2,6},{3,7},{4,0},{5,1},{6,2},{7,3},{8,12},{9,13},{10,... | collective-permute-start | bytes 288824 | tf_op jit(solution)/shard_map/ppermute | solution.py:50
  227.7 4.5 %collective-permute-done.9 = f32[24068]{0:T(1024)S(1)} collective-permute-done((f32[24068]{0:T(1024)S(1)}, f32[24068]{0:T(1024)S(1)}, u32[]{:S(2)}, u32[]{:S(2)}) %collective-permute-start.9) | collective-permute-done | bytes 96304 | tf_op jit(solution)/shard_map/ppermute | solution.py:50
  233.1 4.7 %fusion.16 = bf16[2,64,1536]{2,1,0:T(8,128)(2,1)} fusion(bf16[2,64,1536]{2,1,0:T(8,128)(2,1)S(1)} %fusion.92, bf16[1536,1536]{1,0:T(8,128)(2,1)} %param.15), kind=kOutput, calls=%fused_computation.48 | convolution fusion | flops 604176384 | bytes 5505024 | tf_op jit(solution)/shard_map/dot_general | solution.py:163
  239.7 4.4 %fusion.58 = bf16[2,64,1536]{2,1,0:T(8,128)(2,1)} fusion(bf16[2,64,1536]{2,1,0:T(8,128)(2,1)S(1)} %fusion.19, bf16[2,15,1536]{2,1,0:T(8,128)(2,1)S(1)} %collective-permute-done.1, bf16[2,15,1536]{2,1,0:T(8,128)(2,1)S(1)} %collective-permute-done, f32[1536]{0:T(1024)S(1)} %get-tuple-element.36, f32[1536]{0:T(1024)S(1)} %get-tuple-element.37, ...), kind=kLoop, calls=%fused_computation.142 | loop fusion | flops 35979264 | bytes 1161216 | tf_op jit(solution)/shard_map/convert_element_type | solution.py:151
  (153 shorter events, 37.0 us)
Async XLA Ops:
  0.6 17.7 %copy-start = (bf16[2,64,1536]{2,1,0:T(8,128)(2,1)S(1)}, bf16[2,64,1536]{2,1,0:T(8,128)(2,1)}, u32[]{:S(2)}) copy-start(bf16[2,64,1536]{2,1,0:T(8,128)(2,1)} %param.17) | copy-start | bytes 1179652
  0.6 24.2 %copy-start.3 = (bf16[31,1536]{1,0:T(8,128)(2,1)S(1)}, bf16[31,1536]{1,0:T(8,128)(2,1)}, u32[]{:S(2)}) copy-start(bf16[31,1536]{1,0:T(8,128)(2,1)} %param.16) | copy-start | bytes 285700
  0.7 25.9 %copy-start.28 = (s32[476]{0:T(512)S(1)}, s32[476]{0:T(512)}, u32[]{:S(2)}) copy-start(s32[476]{0:T(512)} %param.19) | copy-start | bytes 5716
  0.7 27.7 %copy-start.30 = (s32[2]{0:T(128)S(1)}, s32[2]{0:T(128)}, u32[]{:S(2)}) copy-start(s32[2]{0:T(128)} %param.14) | copy-start | bytes 28
  0.7 28.9 %copy-start.2 = (s32[23592]{0:T(1024)S(1)}, s32[23592]{0:T(1024)}, u32[]{:S(2)}) copy-start(s32[23592]{0:T(1024)} %param.18) | copy-start | bytes 283108
  7.0 52.7 %all-to-all-start = ((bf16[32,3,64,96]{3,2,1,0:T(8,128)(2,1)}), bf16[32,3,64,96]{3,2,1,0:T(8,128)(2,1)S(1)}, u32[]{:S(2)}, u32[]{:S(2)}) async-start(bf16[32,3,64,96]{3,2,1,0:T(8,128)(2,1)} %bitcast.39), calls=%async_computation | async-start | bytes 3145728 | tf_op jit(solution)/shard_map/all_to_all | solution.py:70
  18.4 37.8 %collective-permute-start.3 = (bf16[2,15,1536]{2,1,0:T(8,128)(2,1)S(1)}, bf16[2,15,1536]{2,1,0:T(8,128)(2,1)S(1)}, u32[]{:S(2)}, u32[]{:S(2)}) collective-permute-start(bf16[2,15,1536]{2,1,0:T(8,128)(2,1)S(1)} %get-tuple-element.74), channel_id=1, source_target_pairs={{1,0},{2,1},{3,2},{4,3},{5,4},{6,5},{7,6},{8,7},{9,8},{10,9},{11,1... | collective-permute-start | bytes 276488 | tf_op jit(solution)/shard_map/ppermute | solution.py:22
  19.7 36.5 %collective-permute-start.2 = (bf16[2,15,1536]{2,1,0:T(8,128)(2,1)S(1)}, bf16[2,15,1536]{2,1,0:T(8,128)(2,1)}, u32[]{:S(2)}, u32[]{:S(2)}) collective-permute-start(bf16[2,15,1536]{2,1,0:T(8,128)(2,1)S(1)} %get-tuple-element.73), channel_id=1, source_target_pairs={{0,1},{1,2},{2,3},{3,4},{4,5},{5,6},{6,7},{7,8},{8,9},{9,10},{10,1... | collective-permute-start | bytes 276488 | tf_op jit(solution)/shard_map/ppermute | solution.py:21
  68.8 11.4 %copy-start.4 = (f32[1536]{0:T(1024)S(1)}, f32[1536]{0:T(1024)}, u32[]{:S(2)}) copy-start(f32[1536]{0:T(1024)} %get-tuple-element.46) | copy-start | bytes 18436
  73.9 23.0 %all-to-all-start.1 = ((bf16[32,64,96]{2,1,0:T(8,128)(2,1)}), bf16[32,64,96]{2,1,0:T(8,128)(2,1)S(1)}, u32[]{:S(2)}, u32[]{:S(2)}) async-start(bf16[32,64,96]{2,1,0:T(8,128)(2,1)} %bitcast.7), calls=%async_computation.1 | async-start | bytes 1048576 | tf_op jit(solution)/shard_map/all_to_all | solution.py:76
  80.4 17.9 %copy-start.1 = (bf16[2,64,1536]{2,1,0:T(8,128)(2,1)S(1)}, bf16[2,64,1536]{2,1,0:T(8,128)(2,1)}, u32[]{:S(2)}) copy-start(bf16[2,64,1536]{2,1,0:T(8,128)(2,1)} %param.13) | copy-start | bytes 1179652
  101.6 94.3 %collective-permute-start.1 = (bf16[2,15,1536]{2,1,0:T(8,128)(2,1)S(1)}, bf16[2,15,1536]{2,1,0:T(8,128)(2,1)S(1)}, u32[]{:S(2)}, u32[]{:S(2)}) collective-permute-start(bf16[2,15,1536]{2,1,0:T(8,128)(2,1)S(1)} %get-tuple-element.76), channel_id=1, source_target_pairs={{1,0},{2,1},{3,2},{4,3},{5,4},{6,5},{7,6},{8,7},{9,8},{10,9},{11,1... | collective-permute-start | bytes 276488 | tf_op jit(solution)/shard_map/ppermute | solution.py:22
  102.9 90.8 %collective-permute-start = (bf16[2,15,1536]{2,1,0:T(8,128)(2,1)S(1)}, bf16[2,15,1536]{2,1,0:T(8,128)(2,1)S(1)}, u32[]{:S(2)}, u32[]{:S(2)}) collective-permute-start(bf16[2,15,1536]{2,1,0:T(8,128)(2,1)S(1)} %get-tuple-element.75), channel_id=1, source_target_pairs={{0,1},{1,2},{2,3},{3,4},{4,5},{5,6},{6,7},{7,8},{8,9},{9,10},{10,1... | collective-permute-start | bytes 276488 | tf_op jit(solution)/shard_map/ppermute | solution.py:21
  171.4 27.2 %copy-start.25 = (s32[1024]{0:T(1024)S(1)}, s32[1024]{0:T(1024)}, u32[]{:S(2)}) copy-start(s32[1024]{0:T(1024)} %pad_clamp_fusion.1) | copy-start | bytes 12292
  171.4 28.4 %copy-start.27 = (s32[476]{0:T(512)S(1)}, s32[476]{0:T(512)}, u32[]{:S(2)}) copy-start(s32[476]{0:T(512)} %add_select_fusion.3) | copy-start | bytes 5716
  171.5 28.4 %copy-start.29 = (pred[476]{0:T(512)(128)(4,1)S(1)}, pred[476]{0:T(512)(128)(4,1)}, u32[]{:S(2)}) copy-start(pred[476]{0:T(512)(128)(4,1)} %get-tuple-element.68) | copy-start | bytes 1432
  200.3 1.3 collective-permute-start.4
  201.7 4.9 %collective-permute-start.5 = (f32[24068]{0:T(1024)S(1)}, f32[24068]{0:T(1024)S(1)}, u32[]{:S(2)}, u32[]{:S(2)}) collective-permute-start(f32[24068]{0:T(1024)S(1)} %fusion.166), channel_id=1, source_target_pairs={{0,64},{32,96},{64,0},{96,32},{128,192},{160,224},{192,128},{224,1... | collective-permute-start | bytes 288824 | tf_op jit(solution)/shard_map/ppermute | solution.py:50
  206.6 6.4 %collective-permute-start.6 = (f32[24068]{0:T(1024)S(1)}, f32[24068]{0:T(1024)S(1)}, u32[]{:S(2)}, u32[]{:S(2)}) collective-permute-start(f32[24068]{0:T(1024)S(1)} %add.326), channel_id=1, source_target_pairs={{0,128},{32,160},{64,192},{96,224},{128,0},{160,32},{192,64},{224,... | collective-permute-start | bytes 288824 | tf_op jit(solution)/shard_map/ppermute | solution.py:50
  213.0 4.7 %collective-permute-start.7 = (f32[24068]{0:T(1024)S(1)}, f32[24068]{0:T(1024)S(1)}, u32[]{:S(2)}, u32[]{:S(2)}) collective-permute-start(f32[24068]{0:T(1024)S(1)} %add.327), channel_id=1, source_target_pairs={{0,1},{1,0},{2,3},{3,2},{4,5},{5,4},{6,7},{7,6},{8,9},{9,8},{10,11... | collective-permute-start | bytes 288824 | tf_op jit(solution)/shard_map/ppermute | solution.py:50
  217.7 5.6 %collective-permute-start.8 = (f32[24068]{0:T(1024)S(1)}, f32[24068]{0:T(1024)S(1)}, u32[]{:S(2)}, u32[]{:S(2)}) collective-permute-start(f32[24068]{0:T(1024)S(1)} %add.328), channel_id=1, source_target_pairs={{0,2},{1,3},{2,0},{3,1},{4,6},{5,7},{6,4},{7,5},{8,10},{9,11},{10,... | collective-permute-start | bytes 288824 | tf_op jit(solution)/shard_map/ppermute | solution.py:50
  223.4 8.9 %collective-permute-start.9 = (f32[24068]{0:T(1024)S(1)}, f32[24068]{0:T(1024)S(1)}, u32[]{:S(2)}, u32[]{:S(2)}) collective-permute-start(f32[24068]{0:T(1024)S(1)} %add.329), channel_id=1, source_target_pairs={{0,4},{1,5},{2,6},{3,7},{4,0},{5,1},{6,2},{7,3},{8,12},{9,13},{10,... | collective-permute-start | bytes 288824 | tf_op jit(solution)/shard_map/ppermute | solution.py:50
  232.2 5.6 %collective-permute-start.10 = (f32[24068]{0:T(1024)S(1)}, f32[24068]{0:T(1024)S(1)}, u32[]{:S(2)}, u32[]{:S(2)}) collective-permute-start(f32[24068]{0:T(1024)S(1)} %add.330), channel_id=1, source_target_pairs={{0,8},{1,9},{2,10},{3,11},{4,12},{5,13},{6,14},{7,15},{8,0},{9,1},... | collective-permute-start | bytes 288824 | tf_op jit(solution)/shard_map/ppermute | solution.py:50
  237.9 6.2 %collective-permute-start.11 = (f32[24068]{0:T(1024)S(1)}, f32[24068]{0:T(1024)S(1)}, u32[]{:S(2)}, u32[]{:S(2)}) collective-permute-start(f32[24068]{0:T(1024)S(1)} %add.331), channel_id=1, source_target_pairs={{0,16},{1,17},{2,18},{3,19},{4,20},{5,21},{6,22},{7,23},{8,24},{9,... | collective-permute-start | bytes 288824 | tf_op jit(solution)/shard_map/ppermute | solution.py:50
  (21 other events, 232.1 us)
